TPU v7x, 32 devices: a whole 2x2x4 slice. The times are simulated.
32 devices in a mesh: src: 8 (over z, core), rcv: 4 (over y, x).
Axes of the slice: x: 2, y: 2, z: 4, core: 2. Of those that a mesh axis runs over, the one named last changes fastest.
Arguments:
- spectra: bfloat16 [128, 4, 2, 2048], P(('src', 'rcv')), may hold values from -50 to 50
- valid: int32 [128, 4], P(('src', 'rcv')), may hold values 0 or 1
Outputs:
- correlations: bfloat16 [128, 128, 512], P('src', 'rcv')
All inputs are finite; a program needn't handle non-finite values. No bound on the sum of `valid` on one device may be relied on, other than what follows from the above.
Results may differ from a plain program's by a relative error of at most 0.0065.
Values may be sent and summed in bfloat16 or wider, within the bound.
No kernel may reach another device: no remote copies, remote signals or barrier semaphores. Data moves between devices by JAX's collectives and lax.ppermute only.
A program may use at most 64 MiB of HBM per device.

v0:
```python
import math
import jax
import jax.numpy as jnp
from jax import lax
from jax.sharding import PartitionSpec as P

LAGS = 512
BAND = 32
NSAMP = 7500
epsilon = 1e-06


def whiten_spectra(spectra):
    values = spectra.astype(jnp.float32)
    squares = values[:, :, 0] ** 2 + values[:, :, 1] ** 2
    banded = squares.reshape(squares.shape[0], squares.shape[1], squares.shape[2] // BAND, BAND)
    power = jnp.sum(banded, axis=3) / (2.0 * BAND)
    factor = jnp.repeat(1.0 / jnp.sqrt(power + epsilon), BAND, axis=2)
    return (values * factor[:, :, None, :]).astype(jnp.bfloat16)


def lag_table(freq_count, lag_count):
    bins_index = jnp.arange(freq_count, dtype=jnp.int32)
    shifts = jnp.arange(lag_count, dtype=jnp.int32) - lag_count // 2
    phase = jnp.mod(bins_index[:, None] * shifts[None, :], NSAMP)
    angle = phase.astype(jnp.float32) * (2.0 * math.pi / NSAMP)
    factor = 1.0 / math.sqrt(2.0 * freq_count)
    cosines = (jnp.cos(angle) * factor).astype(jnp.bfloat16)
    sines = (-jnp.sin(angle) * factor).astype(jnp.bfloat16)
    return jnp.concatenate([cosines, sines], axis=0)


def weighted_cross(rec_spec, rec_mask, src_spec, src_mask):
    counts = jnp.dot(rec_mask, src_mask.T, preferred_element_type=jnp.float32)
    inverse = 1.0 / jnp.maximum(counts, 1.0)
    real_part = jnp.zeros((rec_spec.shape[0], src_spec.shape[0], rec_spec.shape[-1]), jnp.float32)
    imag_part = jnp.zeros_like(real_part)
    for window in range(rec_spec.shape[1]):
        rec_a = rec_spec[:, window, 0].astype(jnp.float32)[:, None, :]
        rec_b = rec_spec[:, window, 1].astype(jnp.float32)[:, None, :]
        src_a = src_spec[:, window, 0].astype(jnp.float32)[None, :, :]
        src_b = src_spec[:, window, 1].astype(jnp.float32)[None, :, :]
        pair_weight = (rec_mask[:, window][:, None] * src_mask[:, window][None, :] * inverse)[
            :, :, None
        ]
        real_part = real_part + pair_weight * (src_a * rec_a + src_b * rec_b)
        imag_part = imag_part + pair_weight * (src_b * rec_a - src_a * rec_b)
    return (real_part, imag_part)


def correlate_block(rec_spec, rec_mask, src_spec, src_mask, table):
    real_part, imag_part = weighted_cross(rec_spec, rec_mask, src_spec, src_mask)
    stacked = jnp.concatenate(
        [real_part.astype(jnp.bfloat16), imag_part.astype(jnp.bfloat16)], axis=2
    )
    return jnp.einsum("iqk,kl->iql", stacked, table, preferred_element_type=jnp.float32)


def group_rows(rec_spec, rec_mask, src_spec, src_mask, table):
    receiver_count = rec_spec.shape[0]
    group_count = receiver_count // 8
    source_masks = src_mask.astype(jnp.float32)

    def one_group(group):
        return correlate_block(
            group[0], group[1].astype(jnp.float32), src_spec, source_masks, table
        ).astype(jnp.bfloat16)

    grouped = (
        rec_spec.reshape((group_count, 8) + rec_spec.shape[1:]),
        rec_mask.reshape(group_count, 8, rec_mask.shape[1]),
    )
    result = lax.map(one_group, grouped)
    return result.reshape(receiver_count, src_spec.shape[0], table.shape[1])


def local(spectra, valid):
    table = lag_table(spectra.shape[-1], LAGS)
    mask_wire = valid.astype(jnp.bfloat16)
    whitened = whiten_spectra(spectra)
    rec_spec, rec_mask = (
        lax.all_gather(whitened, "rcv", axis=0, tiled=True),
        lax.all_gather(mask_wire, "rcv", axis=0, tiled=True),
    )
    portion = lax.all_gather((whitened, mask_wire), "src", axis=0, tiled=True)
    return group_rows(rec_spec, rec_mask, portion[0], portion[1], table)


def solution(mesh):
    return jax.shard_map(
        local,
        mesh=mesh,
        in_specs=(P(("src", "rcv"), None, None, None), P(("src", "rcv"), None)),
        out_specs=P("src", "rcv", None),
        check_vma=False,
    )
```

profile of v0, /device:TPU:0, one launch (start us, length us, event | category | flops | bytes accessed | tf_op | source)
XLA Modules:
  0.0 84.7 jit_solution(15054777667643042789)
XLA Ops:
  6.5 0.0 copy-start.1
  6.5 0.0 copy-start.2
  6.5 0.0 all-gather.4.cloned.1.call-start
  6.5 1.0 %copy_convert_fusion = f32[4,4,2,2048]{3,1,2,0:T(4,128)S(1)} fusion(bf16[4,4,2,2048]{3,2,1,0:T(2,128)(2,1)} %param.4), kind=kLoop, calls=%fused_computation.68 | loop fusion | flops 65536 | bytes 393216 | tf_op jit(solution)/shard_map/convert_element_type | solution.py:14
  7.6 0.2 add.64
  7.8 0.2 reduce_sum.9
  8.0 0.2 broadcast_in_dim.8
  8.3 0.3 mul.164
  8.5 0.0 copy-done.1
  8.5 0.7 multiply_convert_fusion.2
  9.3 0.0 all-gather.4.cloned.1.call-update
  9.3 0.0 copy-done.2
  9.3 9.5 %all-gather = bf16[4,4,4]{2,1,0:T(4,128)(2,1)S(1)} all-gather(bf16[1,4,4]{2,1,0:T(4,128)(2,1)S(1)} %convert_bitcast_fusion), channel_id=1, replica_groups=mesh['src'=8,'rcv'=4] {'rcv'}, dimensions={0}, use_global_device_ids=true | all-gather | bytes 160 | tf_op jit(solution)/shard_map/all_gather | solution.py:83
  18.8 12.0 %all-gather.1 = bf16[8,4,4]{2,1,0:T(4,128)(2,1)S(1)} all-gather(bf16[1,4,4]{2,1,0:T(4,128)(2,1)S(1)} %convert_bitcast_fusion), channel_id=1, replica_groups=mesh['src'=8,'rcv'=4] {'src'}, dimensions={0}, use_global_device_ids=true | all-gather | bytes 288 | tf_op jit(solution)/shard_map/all_gather | solution.py:85
  30.9 0.1 copy.22
  31.0 0.1 copy.23
  31.1 0.1 reshape.163
  31.2 0.1 copy.26
  31.3 10.3 %all_gather.15 = bf16[16,4,2,2048]{3,1,2,0:T(4,128)(2,1)S(1)} all-gather(bf16[4,4,2,2048]{3,1,2,0:T(4,128)(2,1)} %multiply_convert_fusion.2), channel_id=1, replica_groups=mesh['src'=8,'rcv'=4] {'rcv'}, dimensions={0}, use_global_device_ids=true | all-gather | bytes 655360 | tf_op jit(solution)/shard_map/all_gather | solution.py:82
  41.5 17.7 %multiply_convert_fusion.1 = (bf16[2048,512]{1,0:T(8,128)(2,1)S(1)}, bf16[2048,512]{1,0:T(8,128)(2,1)S(1)}) fusion(s32[512]{0:T(512)S(1)} %iota_add_fusion), kind=kLoop, calls=%fused_computation.59 | loop fusion | flops 14680064 | bytes 4196352 | tf_op jit(solution)/shard_map/convert_element_type | solution.py:28
  59.2 2.2 %pad_maximum_fusion = bf16[4096,512]{1,0:T(8,128)(2,1)} fusion(bf16[2048,512]{1,0:T(8,128)(2,1)S(1)} %get-tuple-element.114, bf16[2048,512]{1,0:T(8,128)(2,1)S(1)} %get-tuple-element.113), kind=kLoop, calls=%fused_computation.57 | loop fusion | flops 8388608 | bytes 8388608 | tf_op jit(solution)/shard_map/concatenate | solution.py:30
  61.4 0.0 all-gather.4.cloned.1.call-done
  61.4 1.8 %copy.27 = bf16[32,4,2,2048]{3,0,2,1:T(8,128)(2,1)S(1)} copy(bf16[32,4,2,2048]{3,1,2,0:T(4,128)(2,1)} %all-gather.4.cloned.1.call-done) | data formatting | bytes 2097152 | tf_op jit(solution)/shard_map/while | solution.py:73
  63.2 13.8 %while.10 = (s32[]{:T(128)}, bf16[2,8,32,512]{3,2,1,0:T(8,128)(2,1)S(1)}, bf16[2,8,4]{1,2,0:T(4,128)(2,1)S(1)}, f32[32,4]{0,1:T(4,128)S(1)}, bf16[32,4,2,2048]{3...) while((s32[]{:T(128)}, ...), condition=%wide.region_2.3_spmd, body=%wide.region_1.2_spmd.sunk | while | flops 1099698688 | bytes 35672640 | solution.py:73
  63.3 0.2 multiply_multiply_fusion.5
  63.5 0.1 constant_dynamic-slice_fusion.4
  63.6 0.2 copy.40
  63.8 0.2 bitcast_convert_fusion.11
  64.1 0.0 copy-start
  64.1 2.3 %add_convert_fusion.5 = bf16[8,32,2048]{2,1,0:T(8,128)(2,1)S(1)} fusion(f32[8,2048]{1,0:T(8,128)S(1)} %get-tuple-element.186, f32[32,2048]{1,0:T(8,128)S(1)} %get-tuple-element.187, f32[8,2048]{1,0:T(8,128)S(1)} %get-tuple-element.188, f32[32,2048]{1,0:T(8,128)S(1)} %get-tuple-element.189, f32[8,32]{1,0:T(8,128)S(1)} %get-tuple-element.198, ...), kind=kLoop, calls=%fused_computation.6.clone.1 | loop fusion | flops 10485760 | bytes 3674112 | tf_op jit(solution)/shard_map/while/body/eval_jaxpr/convert_element_type | solution.py:54
  66.4 2.5 %add_convert_fusion.4 = bf16[8,32,2048]{2,1,0:T(8,128)(2,1)S(1)} fusion(f32[8,2048]{1,0:T(8,128)S(1)} %get-tuple-element.186, f32[32,2048]{1,0:T(8,128)S(1)} %get-tuple-element.187, f32[8,2048]{1,0:T(8,128)S(1)} %get-tuple-element.188, f32[32,2048]{1,0:T(8,128)S(1)} %get-tuple-element.189, f32[8,32]{1,0:T(8,128)S(1)} %get-tuple-element.198, ...), kind=kLoop, calls=%fused_computation.5.clone.1 | loop fusion | flops 10485760 | bytes 3674112 | tf_op jit(solution)/shard_map/while/body/eval_jaxpr/convert_element_type | solution.py:54
  68.9 0.0 copy-done
  68.9 1.2 %fusion.47 = bf16[2,8,32,512]{3,2,1,0:T(8,128)(2,1)S(1)} fusion(bf16[2,8,32,512]{3,2,1,0:T(8,128)(2,1)S(1)} %get-tuple-element.223, s32[]{:T(128)} %get-tuple-element.222, bf16[4096,512]{1,0:T(8,128)(2,1)S(1)} %copy-done, bf16[8,32,2048]{2,1,0:T(8,128)(2,1)S(1)} %add_convert_fusion.4, bf16[8,32,2048]{2,1,0:T(8,128)(2,1)S(1)} %add_convert_fusion.5), kind=kOutput, calls=%fused_computation.9.clone.1 | convolution fusion | flops 1078067200 | bytes 6553604 | tf_op jit(solution)/shard_map/while/body/eval_jaxpr/iqk,kl->iql/dot_general | solution.py:56
  70.2 0.2 multiply_multiply_fusion.5
  70.4 0.1 constant_dynamic-slice_fusion.4
  70.5 0.2 copy.40
  70.7 0.2 bitcast_convert_fusion.11
  70.9 0.0 copy-start
  71.0 2.3 %add_convert_fusion.5 = bf16[8,32,2048]{2,1,0:T(8,128)(2,1)S(1)} fusion(f32[8,2048]{1,0:T(8,128)S(1)} %get-tuple-element.186, f32[32,2048]{1,0:T(8,128)S(1)} %get-tuple-element.187, f32[8,2048]{1,0:T(8,128)S(1)} %get-tuple-element.188, f32[32,2048]{1,0:T(8,128)S(1)} %get-tuple-element.189, f32[8,32]{1,0:T(8,128)S(1)} %get-tuple-element.198, ...), kind=kLoop, calls=%fused_computation.6.clone.1 | loop fusion | flops 10485760 | bytes 3674112 | tf_op jit(solution)/shard_map/while/body/eval_jaxpr/convert_element_type | solution.py:54
  73.3 2.5 %add_convert_fusion.4 = bf16[8,32,2048]{2,1,0:T(8,128)(2,1)S(1)} fusion(f32[8,2048]{1,0:T(8,128)S(1)} %get-tuple-element.186, f32[32,2048]{1,0:T(8,128)S(1)} %get-tuple-element.187, f32[8,2048]{1,0:T(8,128)S(1)} %get-tuple-element.188, f32[32,2048]{1,0:T(8,128)S(1)} %get-tuple-element.189, f32[8,32]{1,0:T(8,128)S(1)} %get-tuple-element.198, ...), kind=kLoop, calls=%fused_computation.5.clone.1 | loop fusion | flops 10485760 | bytes 3674112 | tf_op jit(solution)/shard_map/while/body/eval_jaxpr/convert_element_type | solution.py:54
  75.8 0.0 copy-done
  75.8 1.2 %fusion.47 = bf16[2,8,32,512]{3,2,1,0:T(8,128)(2,1)S(1)} fusion(bf16[2,8,32,512]{3,2,1,0:T(8,128)(2,1)S(1)} %get-tuple-element.223, s32[]{:T(128)} %get-tuple-element.222, bf16[4096,512]{1,0:T(8,128)(2,1)S(1)} %copy-done, bf16[8,32,2048]{2,1,0:T(8,128)(2,1)S(1)} %add_convert_fusion.4, bf16[8,32,2048]{2,1,0:T(8,128)(2,1)S(1)} %add_convert_fusion.5), kind=kOutput, calls=%fused_computation.9.clone.1 | convolution fusion | flops 1078067200 | bytes 6553604 | tf_op jit(solution)/shard_map/while/body/eval_jaxpr/iqk,kl->iql/dot_general | solution.py:56
  77.0 0.0 copy-start.3
  77.0 0.8 copy-done.3
  (13 shorter events, 0.2 us)
Async XLA Ops:
  6.5 2.0 %copy-start.1 = (bf16[4,4,2,2048]{3,2,1,0:T(2,128)(2,1)S(1)}, bf16[4,4,2,2048]{3,2,1,0:T(2,128)(2,1)}, u32[]{:S(2)}) copy-start(bf16[4,4,2,2048]{3,2,1,0:T(2,128)(2,1)} %param.4) | copy-start | bytes 393220
  6.5 2.8 %copy-start.2 = (s32[4,4]{1,0:T(4,128)S(1)}, s32[4,4]{1,0:T(4,128)}, u32[]{:S(2)}) copy-start(s32[4,4]{1,0:T(4,128)} %param.5) | copy-start | bytes 196
  6.5 54.9 %all-gather.4.cloned.1.call-start = ((), (), s32[]{:S(2)}) async-start(), calls=%async_computation | async-start | bytes 1179648 | tf_op jit(solution)/shard_map/all_gather | solution.py:85
  64.1 4.8 %copy-start = (bf16[4096,512]{1,0:T(8,128)(2,1)S(1)}, bf16[4096,512]{1,0:T(8,128)(2,1)}, u32[]{:S(2)}) copy-start(bf16[4096,512]{1,0:T(8,128)(2,1)} %get-tuple-element.236) | copy-start | bytes 12582916 | tf_op jit(solution)/shard_map/while
  70.9 4.8 %copy-start = (bf16[4096,512]{1,0:T(8,128)(2,1)S(1)}, bf16[4096,512]{1,0:T(8,128)(2,1)}, u32[]{:S(2)}) copy-start(bf16[4096,512]{1,0:T(8,128)(2,1)} %get-tuple-element.236) | copy-start | bytes 12582916 | tf_op jit(solution)/shard_map/while
  77.0 0.8 copy-start.3
Sparse Core Ops, SparseCore 0:
  9.4 24.8 all-gather.3
where the time goes:
time: 84.9 us; the launch traced here: 84.7 us
  other arithmetic  32.1 us (38%)
  blocking collectives  31.8 us (37%)
  between operations  13.5 us (16%)
  local copies, waits for them, and re-layouts  4.24 us (5%)
  matrix products  2.84 us (3%)
    convert_element_type x1, other arithmetic, lag_table(): cosines = (jnp.cos(angle) * factor).astype(jnp.bfloat16)  17.7 us
    all_gather x1, blocking collectives, local(): portion = lax.all_gather((whitened, mask_wire), 'src', axis=0, tiled=True)  12 us
    all_gather x1, blocking collectives, local(): lax.all_gather(whitened, 'rcv', axis=0, tiled=True)  10.3 us
    all_gather x1, blocking collectives, local(): lax.all_gather(mask_wire, 'rcv', axis=0, tiled=True)  9.52 us
    convert_element_type x2, other arithmetic, correlate_block(): imag_part.astype(jnp.bfloat16)  4.96 us
    convert_element_type x2, other arithmetic, correlate_block(): real_part.astype(jnp.bfloat16)  4.61 us
    dot_general x2, matrix products, correlate_block(): jnp.einsum('iqk,kl->iql', stacked, table, preferred_element_type=jnp.floa...  2.49 us
    concatenate x1, other arithmetic, lag_table(): return jnp.concatenate([cosines, sines], axis=0)  2.23 us
  transfers between devices with their start and end apart: 1, of which 0 were waited for; matrix products, arithmetic and copies ran while one was open for 24% of the time, Pallas kernels for 0%

commit v1 on v0

--- a/solution.py
+++ b/solution.py
@@ -8,6 +8,20 @@
 BAND = 32
 NSAMP = 7500
 epsilon = 1e-06
+
+
+def _direct_boxes(local_array, along_axis):
+    outcome_arr, part_next = (lax.axis_size(along_axis), lax.axis_index(along_axis))
+    fresh, known = (local_array, 1)
+    while known < outcome_arr:
+        block_now = lax.ppermute(
+            fresh, along_axis, perm=[(i0, i0 ^ known) for i0 in range(outcome_arr)]
+        )
+        k_now = jnp.concatenate([fresh, block_now], 0)
+        f_now = jnp.concatenate([block_now, fresh], 0)
+        fresh = jnp.where(part_next & known == 0, k_now, f_now)
+        known = 2 * known
+    return fresh
 
 
 def whiten_spectra(spectra):
@@ -79,7 +93,7 @@
     mask_wire = valid.astype(jnp.bfloat16)
     whitened = whiten_spectra(spectra)
     rec_spec, rec_mask = (
-        lax.all_gather(whitened, "rcv", axis=0, tiled=True),
+        _direct_boxes(whitened, "rcv"),
         lax.all_gather(mask_wire, "rcv", axis=0, tiled=True),
     )
     portion = lax.all_gather((whitened, mask_wire), "src", axis=0, tiled=True)

time: 84.9 us -> 77 us (0.907)
  blocking collectives: 31.8 us -> 19 us
  starting transfers between devices: 0.01 us -> 4.59 us
    all_gather x1 -> x0, blocking collectives: 10.3 us -> none  [local(): lax.all_gather(whitened, 'rcv', axis=0, tiled=True)]
    ppermute x0 -> x2, starting transfers between devices: none -> 4.59 us  [_direct_boxes(): lax.ppermute(fresh, along_axis, perm=[(i0, i0 ^ known) for i0 in range(ou...]
    all_gather x1, blocking collectives: 9.52 us -> 7.07 us  [local(): lax.all_gather(mask_wire, 'rcv', axis=0, tiled=True)]
  transfers between devices with their start and end apart: 1 -> 3, of which waited for: 0 -> 0; matrix products, arithmetic and copies ran while one was open for 24% -> 28% of each run, Pallas kernels for 0% -> 0%
where the time goes in v1:
time: 77 us; the launch traced here: 76.8 us
  other arithmetic  31.8 us (41%)
  blocking collectives  19 us (25%)
  between operations  13.6 us (18%)
  local copies, waits for them, and re-layouts  4.7 us (6%)
  starting transfers between devices  4.59 us (6%)
  matrix products  2.84 us (4%)
    convert_element_type x1, other arithmetic, lag_table(): cosines = (jnp.cos(angle) * factor).astype(jnp.bfloat16)  17.7 us
    all_gather x1, blocking collectives, local(): portion = lax.all_gather((whitened, mask_wire), 'src', axis=0, tiled=True)  12 us
    all_gather x1, blocking collectives, local(): lax.all_gather(mask_wire, 'rcv', axis=0, tiled=True)  7.07 us
    convert_element_type x2, other arithmetic, correlate_block(): imag_part.astype(jnp.bfloat16)  4.96 us
    convert_element_type x2, other arithmetic, correlate_block(): real_part.astype(jnp.bfloat16)  4.61 us
    ppermute x2, starting transfers between devices, _direct_boxes(): lax.ppermute(fresh, along_axis, perm=[(i0, i0 ^ known) for i0 in range(ou...  4.59 us
    dot_general x2, matrix products, correlate_block(): jnp.einsum('iqk,kl->iql', stacked, table, preferred_element_type=jnp.floa...  2.49 us
    concatenate x1, other arithmetic, lag_table(): return jnp.concatenate([cosines, sines], axis=0)  2.22 us
  transfers between devices with their start and end apart: 3, of which 0 were waited for; matrix products, arithmetic and copies ran while one was open for 28% of the time, Pallas kernels for 0%

profile of v1, /device:TPU:0, one launch (start us, length us, event | category | flops | bytes accessed | tf_op | source)
XLA Modules:
  0.0 76.8 jit_solution(638116735908146343)
XLA Ops:
  6.5 0.0 copy-start.1
  6.5 0.0 all-gather.4.cloned.1.call-start
  6.5 1.1 %copy_convert_fusion = f32[4,4,2,2048]{3,0,2,1:T(4,128)S(1)} fusion(bf16[4,4,2,2048]{3,2,1,0:T(2,128)(2,1)} %param.4), kind=kLoop, calls=%fused_computation.70 | loop fusion | flops 65536 | bytes 393216 | tf_op jit(solution)/shard_map/convert_element_type | solution.py:28
  7.7 0.1 copy.27
  7.8 0.2 add.64
  7.9 0.2 reduce_sum.9
  8.2 0.2 broadcast_in_dim.8
  8.4 0.3 mul.164
  8.7 0.1 copy.28
  8.7 0.0 copy-done.1
  8.8 0.1 multiply_convert_fusion.2
  8.9 3.0 %collective-permute-start = (bf16[4,4,2,2048]{3,0,2,1:T(4,128)(2,1)S(1)}, bf16[4,4,2,2048]{3,0,2,1:T(4,128)(2,1)S(1)}, u32[]{:S(2)}, u32[]{:S(2)}) collective-permute-start(bf16[4,4,2,2048]{3,0,2,1:T(4,128)(2,1)S(1)} %multiply_convert_fusion.2), channel_id=1, source_target_pairs={{0,1},{1,0},{2,3},{3,2},{4,5},{5,4},{6,7},{7,6},{8,9},{9,8},{10,11... | collective-permute-start | bytes 393224 | tf_op jit(solution)/shard_map/ppermute | solution.py:17
  11.9 0.8 copy.29
  12.6 0.0 all-gather.4.cloned.1.call-update
  12.7 0.0 copy-start.2
  12.7 17.7 %multiply_convert_fusion.1 = (bf16[2048,512]{1,0:T(8,128)(2,1)S(1)}, bf16[2048,512]{1,0:T(8,128)(2,1)S(1)}) fusion(s32[512]{0:T(512)S(1)} %iota_add_fusion), kind=kLoop, calls=%fused_computation.58 | loop fusion | flops 14680064 | bytes 4196352 | tf_op jit(solution)/shard_map/convert_element_type | solution.py:42
  30.4 0.0 copy-done.2
  30.4 0.0 collective-permute-done
  30.4 0.2 maximum_select_fusion.1
  30.6 1.6 %collective-permute-start.1 = (bf16[8,4,2,2048]{3,0,2,1:T(8,128)(2,1)S(1)}, bf16[8,4,2,2048]{3,0,2,1:T(8,128)(2,1)S(1)}, u32[]{:S(2)}, u32[]{:S(2)}) collective-permute-start(bf16[8,4,2,2048]{3,0,2,1:T(8,128)(2,1)S(1)} %maximum_select_fusion.1), channel_id=1, source_target_pairs={{0,2},{1,3},{2,0},{3,1},{4,6},{5,7},{6,4},{7,5},{8,10},{9,11},{10,... | collective-permute-start | bytes 786440 | tf_op jit(solution)/shard_map/ppermute | solution.py:17
  32.2 2.2 %pad_maximum_fusion = bf16[4096,512]{1,0:T(8,128)(2,1)} fusion(bf16[2048,512]{1,0:T(8,128)(2,1)S(1)} %get-tuple-element.114, bf16[2048,512]{1,0:T(8,128)(2,1)S(1)} %get-tuple-element.113), kind=kLoop, calls=%fused_computation.56 | loop fusion | flops 8388608 | bytes 8388608 | tf_op jit(solution)/shard_map/concatenate | solution.py:44
  34.4 7.1 %all-gather = bf16[4,4,4]{2,1,0:T(4,128)(2,1)S(1)} all-gather(bf16[1,4,4]{2,1,0:T(4,128)(2,1)S(1)} %convert_bitcast_fusion), channel_id=1, replica_groups=mesh['src'=8,'rcv'=4] {'rcv'}, dimensions={0}, use_global_device_ids=true | all-gather | bytes 160 | tf_op jit(solution)/shard_map/all_gather | solution.py:97
  41.5 12.0 %all-gather.1 = bf16[8,4,4]{2,1,0:T(4,128)(2,1)S(1)} all-gather(bf16[1,4,4]{2,1,0:T(4,128)(2,1)S(1)} %convert_bitcast_fusion), channel_id=1, replica_groups=mesh['src'=8,'rcv'=4] {'src'}, dimensions={0}, use_global_device_ids=true | all-gather | bytes 288 | tf_op jit(solution)/shard_map/all_gather | solution.py:99
  53.5 0.1 copy.24
  53.6 0.1 copy.25
  53.7 0.1 reshape.164
  53.8 0.1 copy.30
  53.9 0.0 collective-permute-done.1
  53.9 0.1 fusion.36
  54.0 0.0 all-gather.4.cloned.1.call-done
  54.0 1.8 %copy.31 = bf16[32,4,2,2048]{3,0,2,1:T(8,128)(2,1)S(1)} copy(bf16[32,4,2,2048]{3,1,2,0:T(4,128)(2,1)} %all-gather.4.cloned.1.call-done) | data formatting | bytes 2097152 | tf_op jit(solution)/shard_map/while | solution.py:87
  55.9 13.3 %while.10 = (s32[]{:T(128)}, bf16[2,8,32,512]{3,2,1,0:T(8,128)(2,1)S(1)}, bf16[2,8,4]{1,2,0:T(4,128)(2,1)S(1)}, f32[32,4]{0,1:T(4,128)S(1)}, bf16[32,4,2,2048]{3...) while((s32[]{:T(128)}, ...), condition=%wide.region_2.3_spmd, body=%wide.region_1.2_spmd.sunk | while | flops 1099698688 | bytes 35148352 | solution.py:87
  55.9 0.2 multiply_multiply_fusion.5
  56.2 0.2 bitcast_convert_fusion.11
  56.4 0.0 copy-start
  56.4 2.3 %add_convert_fusion.5 = bf16[8,32,2048]{2,1,0:T(8,128)(2,1)S(1)} fusion(f32[8,2048]{1,0:T(8,128)S(1)} %get-tuple-element.186, f32[32,2048]{1,0:T(8,128)S(1)} %get-tuple-element.187, f32[8,2048]{1,0:T(8,128)S(1)} %get-tuple-element.188, f32[32,2048]{1,0:T(8,128)S(1)} %get-tuple-element.189, f32[8,32]{1,0:T(8,128)S(1)} %get-tuple-element.198, ...), kind=kLoop, calls=%fused_computation.6.clone.1 | loop fusion | flops 10485760 | bytes 3674112 | tf_op jit(solution)/shard_map/while/body/eval_jaxpr/convert_element_type | solution.py:68
  58.7 2.5 %add_convert_fusion.4 = bf16[8,32,2048]{2,1,0:T(8,128)(2,1)S(1)} fusion(f32[8,2048]{1,0:T(8,128)S(1)} %get-tuple-element.186, f32[32,2048]{1,0:T(8,128)S(1)} %get-tuple-element.187, f32[8,2048]{1,0:T(8,128)S(1)} %get-tuple-element.188, f32[32,2048]{1,0:T(8,128)S(1)} %get-tuple-element.189, f32[8,32]{1,0:T(8,128)S(1)} %get-tuple-element.198, ...), kind=kLoop, calls=%fused_computation.5.clone.1 | loop fusion | flops 10485760 | bytes 3674112 | tf_op jit(solution)/shard_map/while/body/eval_jaxpr/convert_element_type | solution.py:68
  61.2 0.0 copy-done
  61.2 1.2 %fusion.48 = bf16[2,8,32,512]{3,2,1,0:T(8,128)(2,1)S(1)} fusion(bf16[2,8,32,512]{3,2,1,0:T(8,128)(2,1)S(1)} %get-tuple-element.223, s32[]{:T(128)} %get-tuple-element.222, bf16[4096,512]{1,0:T(8,128)(2,1)S(1)} %copy-done, bf16[8,32,2048]{2,1,0:T(8,128)(2,1)S(1)} %add_convert_fusion.4, bf16[8,32,2048]{2,1,0:T(8,128)(2,1)S(1)} %add_convert_fusion.5), kind=kOutput, calls=%fused_computation.9.clone.1 | convolution fusion | flops 1078067200 | bytes 6553604 | tf_op jit(solution)/shard_map/while/body/eval_jaxpr/iqk,kl->iql/dot_general | solution.py:70
  62.5 0.2 multiply_multiply_fusion.5
  62.8 0.2 bitcast_convert_fusion.11
  63.1 0.0 copy-start
  63.1 2.3 %add_convert_fusion.5 = bf16[8,32,2048]{2,1,0:T(8,128)(2,1)S(1)} fusion(f32[8,2048]{1,0:T(8,128)S(1)} %get-tuple-element.186, f32[32,2048]{1,0:T(8,128)S(1)} %get-tuple-element.187, f32[8,2048]{1,0:T(8,128)S(1)} %get-tuple-element.188, f32[32,2048]{1,0:T(8,128)S(1)} %get-tuple-element.189, f32[8,32]{1,0:T(8,128)S(1)} %get-tuple-element.198, ...), kind=kLoop, calls=%fused_computation.6.clone.1 | loop fusion | flops 10485760 | bytes 3674112 | tf_op jit(solution)/shard_map/while/body/eval_jaxpr/convert_element_type | solution.py:68
  65.4 2.5 %add_convert_fusion.4 = bf16[8,32,2048]{2,1,0:T(8,128)(2,1)S(1)} fusion(f32[8,2048]{1,0:T(8,128)S(1)} %get-tuple-element.186, f32[32,2048]{1,0:T(8,128)S(1)} %get-tuple-element.187, f32[8,2048]{1,0:T(8,128)S(1)} %get-tuple-element.188, f32[32,2048]{1,0:T(8,128)S(1)} %get-tuple-element.189, f32[8,32]{1,0:T(8,128)S(1)} %get-tuple-element.198, ...), kind=kLoop, calls=%fused_computation.5.clone.1 | loop fusion | flops 10485760 | bytes 3674112 | tf_op jit(solution)/shard_map/while/body/eval_jaxpr/convert_element_type | solution.py:68
  67.9 0.0 copy-done
  67.9 1.2 %fusion.48 = bf16[2,8,32,512]{3,2,1,0:T(8,128)(2,1)S(1)} fusion(bf16[2,8,32,512]{3,2,1,0:T(8,128)(2,1)S(1)} %get-tuple-element.223, s32[]{:T(128)} %get-tuple-element.222, bf16[4096,512]{1,0:T(8,128)(2,1)S(1)} %copy-done, bf16[8,32,2048]{2,1,0:T(8,128)(2,1)S(1)} %add_convert_fusion.4, bf16[8,32,2048]{2,1,0:T(8,128)(2,1)S(1)} %add_convert_fusion.5), kind=kOutput, calls=%fused_computation.9.clone.1 | convolution fusion | flops 1078067200 | bytes 6553604 | tf_op jit(solution)/shard_map/while/body/eval_jaxpr/iqk,kl->iql/dot_general | solution.py:70
  69.1 0.0 copy-start.3
  69.1 0.8 %copy-done.3 = bf16[2,8,32,512]{3,2,1,0:T(8,128)(2,1)} copy-done((bf16[2,8,32,512]{3,2,1,0:T(8,128)(2,1)}, bf16[2,8,32,512]{3,2,1,0:T(8,128)(2,1)S(1)}, u32[]{:S(2)}) %copy-start.3) | copy-done | bytes 524312
  (15 shorter events, 0.3 us)
Async XLA Ops:
  6.5 2.2 %copy-start.1 = (bf16[4,4,2,2048]{3,2,1,0:T(2,128)(2,1)S(1)}, bf16[4,4,2,2048]{3,2,1,0:T(2,128)(2,1)}, u32[]{:S(2)}) copy-start(bf16[4,4,2,2048]{3,2,1,0:T(2,128)(2,1)} %param.4) | copy-start | bytes 393220
  6.5 47.5 %all-gather.4.cloned.1.call-start = ((), (), s32[]{:S(2)}) async-start(), calls=%async_computation | async-start | bytes 1179648 | tf_op jit(solution)/shard_map/all_gather | solution.py:99
  8.9 21.5 %collective-permute-start = (bf16[4,4,2,2048]{3,0,2,1:T(4,128)(2,1)S(1)}, bf16[4,4,2,2048]{3,0,2,1:T(4,128)(2,1)S(1)}, u32[]{:S(2)}, u32[]{:S(2)}) collective-permute-start(bf16[4,4,2,2048]{3,0,2,1:T(4,128)(2,1)S(1)} %multiply_convert_fusion.2), channel_id=1, source_target_pairs={{0,1},{1,0},{2,3},{3,2},{4,5},{5,4},{6,7},{7,6},{8,9},{9,8},{10,11... | collective-permute-start | bytes 393224 | tf_op jit(solution)/shard_map/ppermute | solution.py:17
  12.7 17.7 %copy-start.2 = (s32[4,4]{1,0:T(4,128)S(1)}, s32[4,4]{1,0:T(4,128)}, u32[]{:S(2)}) copy-start(s32[4,4]{1,0:T(4,128)} %param.5) | copy-start | bytes 196
  30.6 23.3 %collective-permute-start.1 = (bf16[8,4,2,2048]{3,0,2,1:T(8,128)(2,1)S(1)}, bf16[8,4,2,2048]{3,0,2,1:T(8,128)(2,1)S(1)}, u32[]{:S(2)}, u32[]{:S(2)}) collective-permute-start(bf16[8,4,2,2048]{3,0,2,1:T(8,128)(2,1)S(1)} %maximum_select_fusion.1), channel_id=1, source_target_pairs={{0,2},{1,3},{2,0},{3,1},{4,6},{5,7},{6,4},{7,5},{8,10},{9,11},{10,... | collective-permute-start | bytes 786440 | tf_op jit(solution)/shard_map/ppermute | solution.py:17
  56.4 4.8 %copy-start = (bf16[4096,512]{1,0:T(8,128)(2,1)S(1)}, bf16[4096,512]{1,0:T(8,128)(2,1)}, u32[]{:S(2)}) copy-start(bf16[4096,512]{1,0:T(8,128)(2,1)} %get-tuple-element.236) | copy-start | bytes 12582916 | tf_op jit(solution)/shard_map/while
  63.1 4.8 %copy-start = (bf16[4096,512]{1,0:T(8,128)(2,1)S(1)}, bf16[4096,512]{1,0:T(8,128)(2,1)}, u32[]{:S(2)}) copy-start(bf16[4096,512]{1,0:T(8,128)(2,1)} %get-tuple-element.236) | copy-start | bytes 12582916 | tf_op jit(solution)/shard_map/while
  69.1 0.8 %copy-start.3 = (bf16[2,8,32,512]{3,2,1,0:T(8,128)(2,1)}, bf16[2,8,32,512]{3,2,1,0:T(8,128)(2,1)S(1)}, u32[]{:S(2)}) copy-start(bf16[2,8,32,512]{3,2,1,0:T(8,128)(2,1)S(1)} %get-tuple-element.42) | copy-start | bytes 1572868
Sparse Core Ops, SparseCore 0:
  12.8 22.4 all-gather.3
